TPU v7x, 512 devices: a whole 4x8x8 slice. The times are simulated.
512 devices in a mesh: box: 64 (over x, y, z_hi), row: 8 (over z_lo, core).
Axes of the slice: x: 4, y: 8, z: 8 (z_hi: 2, z_lo: 4; z = z_hi * 4 + z_lo), core: 2. Of those that a mesh axis runs over, the one named last changes fastest.
Arguments:
- leaf_maps: float32 [64, 2048, 2048], P('box', 'row'), as said below
- iface_index: int32 [64, 512], replicated, may hold values from 0 to 511, as said below
Outputs:
- merged_maps: bfloat16 [64, 2048, 3072], P('box', 'row')
Inputs may be any that keep to these rules, and one draw needn't show every extreme that they name: Each row of iface_index is a permutation of 0 .. 511. Each leaf_maps[c] is exactly symmetric.
All inputs are finite; a program needn't handle non-finite values.
Results may differ from a plain program's by a relative error of at most 0.001.
Values sent between devices are 32-bit elements; how exact they have to be, the bound alone decides.
No kernel may reach another device: no remote copies, remote signals or barrier semaphores. Data moves between devices by JAX's collectives and lax.ppermute only.
A program may use at most 64 MiB of HBM per device.

v0:
```python
import jax
import jax.numpy as jnp
from jax import lax
from jax.sharding import PartitionSpec as P


def swapped(value, axis, stride):
    mask = 2**stride
    pairs = [(source, source ^ mask) for source in range(lax.axis_size(axis))]
    return lax.ppermute(value, axis, pairs)


def body(leaf_maps, iface_index):
    local = leaf_maps[0]
    rows_here = local.shape[0]
    width = local.shape[1]
    inner = iface_index.shape[1]
    outer = width - inner
    box_id = lax.axis_index("box")
    is_first = box_id % 2 == 0
    partner_id = box_id + 1 - 2 * (box_id % 2)
    own_index = lax.dynamic_index_in_dim(iface_index, box_id, 0, keepdims=False)
    partner_index = lax.dynamic_index_in_dim(iface_index, partner_id, 0, keepdims=False)
    mine = jnp.take(local[:, outer:], own_index, axis=1)
    own_full = lax.all_gather(mine, "row", axis=0, tiled=True)
    other_full = swapped(own_full, "box", 0)
    schur = jnp.take(own_full[outer:], own_index, axis=0) + jnp.take(
        other_full[outer:], partner_index, axis=0
    )
    squared = jnp.dot(schur, schur, precision=lax.Precision.HIGHEST)
    factor = jnp.linalg.cholesky(squared)
    first_ext = jnp.where(is_first, own_full[:outer], other_full[:outer])
    second_ext = jnp.where(is_first, other_full[:outer], own_full[:outer])
    global_rows = lax.axis_index("row") * rows_here + jnp.arange(rows_here, dtype=jnp.int32)
    unit = (own_index[None, :] == (global_rows - outer)[:, None]).astype(jnp.float32)
    replaced = jnp.logical_and(is_first, global_rows >= outer)
    left = jnp.where(replaced[:, None], unit, mine)
    local_ext = local[:, :outer]
    zero = jnp.zeros((), jnp.float32)
    left_part = jnp.where(jnp.logical_and(is_first, global_rows < outer)[:, None], local_ext, zero)
    right_part = jnp.where(is_first, zero, local_ext)
    base = jnp.concatenate([left_part, right_part], 1)
    turned = jnp.dot(schur, left.T, precision=lax.Precision.HIGHEST)
    solved = jax.scipy.linalg.cho_solve((factor, True), turned).T
    contract = (((1,), (1,)), ((), ()))
    update_first = lax.dot_general(solved, first_ext, contract, precision=lax.Precision.HIGHEST)
    update_second = lax.dot_general(solved, second_ext, contract, precision=lax.Precision.HIGHEST)
    merged = base - jnp.concatenate([update_first, update_second], 1)
    return merged.astype(jnp.bfloat16)[None]


def solution(mesh):
    in_specs = (P("box", "row", None), P())
    out_specs = P("box", "row", None)
    return jax.shard_map(body, mesh=mesh, in_specs=in_specs, out_specs=out_specs, check_vma=False)
```

profile of v0, /device:TPU:4, one launch (start us, length us, event | category | flops | bytes accessed | tf_op | source)
XLA Modules:
  0.0 439.9 jit_solution(11699187846083616787)
XLA Ops:
  9.3 1.6 gather_fusion
  11.9 62.4 %all-gather.2.cloned.1.call-done = f32[2048,512]{0,1:T(8,128)} async-done(((f32[256,512]{0,1:T(8,128)}), f32[2048,512]{0,1:T(8,128)}) %all-gather.2.cloned.1.call-update) | async-done | bytes 4194320 | tf_op jit(solution)/shard_map/all_gather | solution.py:25
  74.2 5.3 %collective-permute-start = (f32[2048,512]{0,1:T(8,128)}, f32[2048,512]{0,1:T(8,128)}, u32[]{:S(2)}, u32[]{:S(2)}) collective-permute-start(f32[2048,512]{0,1:T(8,128)} %all-gather.2.cloned.1.call-done), channel_id=1, source_target_pairs={{0,8},{8,0},{16,24},{24,16},{32,40},{40,32},{48,56},{56,48},{64,72... | collective-permute-start | bytes 12582920 | tf_op jit(solution)/shard_map/ppermute | solution.py:10
  79.7 1.9 select_bitcast_fusion.1
  81.5 1.3 slice.192
  83.2 1.6 gather_fusion.1
  84.8 177.5 %collective-permute-done = f32[2048,512]{0,1:T(8,128)} collective-permute-done((f32[2048,512]{0,1:T(8,128)}, f32[2048,512]{0,1:T(8,128)}, u32[]{:S(2)}, u32[]{:S(2)}) %collective-permute-start) | collective-permute-done | bytes 4194336 | tf_op jit(solution)/shard_map/ppermute | solution.py:10
  262.3 1.3 slice.193
  263.9 2.1 gather_fusion.2
  266.0 2.2 fusion.74
  268.2 1.3 copy.10
  269.5 1.4 fusion.17
  272.0 11.7 %cholesky.104 = f32[128,128]{1,0:T(8,128)S(1)} custom-call(f32[128,128]{1,0:T(8,128)S(1)} %cholesky.266), custom_call_target="Cholesky" | custom-call | tf_op jit(solution)/shard_map/jit(cholesky)/cholesky | solution.py:31
  283.9 9.8 %custom-call.34 = f32[1,128,128]{1,2,0:T(8,128)S(1)} custom-call(f32[1,128,128]{2,1,0:T(8,128)S(1)} %get-tuple-element.37), custom_call_target="InvertDiagBlocksLowerTriangular" | custom-call | tf_op jit(solution)/shard_map/jit(cholesky)/cholesky | solution.py:31
  293.7 1.2 constant_dynamic-update-slice_fusion.2
  294.9 1.3 convolution_subtract_fusion
  296.2 11.9 %cholesky.217 = f32[128,128]{1,0:T(8,128)S(1)} custom-call(f32[128,128]{1,0:T(8,128)S(1)} %cholesky.270), custom_call_target="Cholesky" | custom-call | tf_op jit(solution)/shard_map/jit(cholesky)/cholesky | solution.py:31
  309.4 9.8 %custom-call.35 = f32[1,128,128]{1,2,0:T(8,128)S(1)} custom-call(f32[1,128,128]{2,1,0:T(8,128)S(1)} %get-tuple-element.34), custom_call_target="InvertDiagBlocksLowerTriangular" | custom-call | tf_op jit(solution)/shard_map/jit(cholesky)/cholesky | solution.py:31
  319.5 1.3 convolution_subtract_fusion.5
  320.8 11.7 %cholesky.238 = f32[128,128]{1,0:T(8,128)S(1)} custom-call(f32[128,128]{1,0:T(8,128)S(1)} %cholesky.275), custom_call_target="Cholesky" | custom-call | tf_op jit(solution)/shard_map/jit(cholesky)/cholesky | solution.py:31
  333.2 9.8 %custom-call.36 = f32[1,128,128]{1,2,0:T(8,128)S(1)} custom-call(f32[1,128,128]{2,1,0:T(8,128)S(1)} %get-tuple-element.31), custom_call_target="InvertDiagBlocksLowerTriangular" | custom-call | tf_op jit(solution)/shard_map/jit(cholesky)/cholesky | solution.py:31
  344.5 11.9 %cholesky.255 = f32[128,128]{1,0:T(8,128)S(1)} custom-call(f32[128,128]{1,0:T(8,128)S(1)} %convolution_subtract_fusion.8), custom_call_target="Cholesky" | custom-call | tf_op jit(solution)/shard_map/jit(cholesky)/cholesky | solution.py:31
  360.6 14.0 %while.1 = (s32[]{:T(128)}, f32[512,512]{1,0:T(8,128)}, s32[4,2]{0,1:T(2,128)S(1)}, f32[4,128,128]{2,1,0:T(8,128)}, s32[]{:T(128)}) while((s32[]{:T(128)}, f32[512,512]{1,0:T(8,128)}, s32[4,2]{0,1:T(2,128)S(1)}, f32[4,128,128]{2,1,0:T(8,128)}, s32[]{:T(128)}) %tuple.31), condition=%wide.while_cond, body=%wide.while_body.sunk | while | flops 2 | bytes 132705 | solution.py:44
  361.2 2.9 bitcast_dynamic-update-slice_fusion.2
  364.7 2.9 bitcast_dynamic-update-slice_fusion.2
  368.2 2.9 bitcast_dynamic-update-slice_fusion.2
  371.7 2.8 bitcast_dynamic-update-slice_fusion.2
  374.5 40.2 %custom-call.37 = f32[4,128,128]{1,2,0:T(8,128)S(1)} custom-call(f32[4,128,128]{2,1,0:T(8,128)} %get-tuple-element.13), custom_call_target="InvertDiagBlocksLowerTriangular" | custom-call | tf_op jit(solution)/shard_map/jit(_cho_solve)/triangular_solve | solution.py:44
  414.7 2.3 fusion.18
  421.6 4.8 %fusion.9 = f32[1,256,1536]{2,1,0:T(8,128)S(1)} fusion(f32[2048,512]{0,1:T(8,128)} %collective-permute-done, f32[2048,512]{0,1:T(8,128)S(1)} %copy-done, pred[]{:T(512)S(6)} %eq.19, f32[128,256]{1,0:T(8,128)S(1)} %fusion.65, f32[128,256]{1,0:T(8,128)S(1)} %fusion.63, f32[128,256]{1,0:T(8,128)S(1)} %fusion.61, f32[128,256]{1,0:T(8,128)S(1)} %fusion.60), kind=kOutput, calls=%fused_computation.15 | convolution fusion | flops 2417098752 | bytes 8388609 | tf_op jit(solution)/shard_map/dot_general | solution.py:46
  426.4 4.9 %fusion.12 = f32[1,256,1536]{2,1,0:T(8,128)S(1)} fusion(f32[2048,512]{0,1:T(8,128)} %collective-permute-done, f32[2048,512]{0,1:T(8,128)S(1)} %copy-done, pred[]{:T(512)S(6)} %eq.19, f32[128,256]{1,0:T(8,128)S(1)} %fusion.65, f32[128,256]{1,0:T(8,128)S(1)} %fusion.63, f32[128,256]{1,0:T(8,128)S(1)} %fusion.61, f32[128,256]{1,0:T(8,128)S(1)} %fusion.60), kind=kOutput, calls=%fused_computation.16 | convolution fusion | flops 2417098752 | bytes 8388609 | tf_op jit(solution)/shard_map/dot_general | solution.py:47
  431.3 1.5 fusion
  (72 shorter events, 18.0 us)
Async XLA Ops:
  6.5 67.7 %all-gather.2.cloned.1.call-start = ((), (), s32[]{:S(2)}) async-start(), calls=%async_computation | async-start | bytes 4718592 | tf_op jit(solution)/shard_map/all_gather | solution.py:25
  9.3 70.4 %copy-start.6 = (f32[1,256,2048]{2,1,0:T(8,128)S(1)}, f32[1,256,2048]{2,1,0:T(8,128)}, u32[]{:S(2)}) copy-start(f32[1,256,2048]{2,1,0:T(8,128)} %param.4) | copy-start | bytes 6291460
  10.9 70.7 %copy-start.3 = (f32[512,256]{1,0:T(8,128)}, f32[512,256]{1,0:T(8,128)S(1)}, u32[]{:S(2)}) copy-start(f32[512,256]{1,0:T(8,128)S(1)} %gather_fusion) | copy-start | bytes 1572868
  74.2 188.0 %collective-permute-start = (f32[2048,512]{0,1:T(8,128)}, f32[2048,512]{0,1:T(8,128)}, u32[]{:S(2)}, u32[]{:S(2)}) collective-permute-start(f32[2048,512]{0,1:T(8,128)} %all-gather.2.cloned.1.call-done), channel_id=1, source_target_pairs={{0,8},{8,0},{16,24},{24,16},{32,40},{40,32},{48,56},{56,48},{64,72... | collective-permute-start | bytes 12582920 | tf_op jit(solution)/shard_map/ppermute | solution.py:10
  271.0 1.0 copy-start.5
  374.5 42.8 %copy-start.4 = (f32[512,512]{1,0:T(8,128)S(1)}, f32[512,512]{1,0:T(8,128)}, u32[]{:S(2)}) copy-start(f32[512,512]{1,0:T(8,128)} %get-tuple-element.91) | copy-start | bytes 3145732
  417.3 4.2 copy-start
  426.4 4.9 %copy-start.1 = (f32[1,256,1536]{2,1,0:T(8,128)S(1)}, f32[1,256,1536]{2,1,0:T(8,128)}, u32[]{:S(2)}) copy-start(f32[1,256,1536]{2,1,0:T(8,128)} %get-tuple-element.26) | copy-start | bytes 4718596
  426.4 4.9 %copy-start.2 = (f32[1,256,1536]{2,1,0:T(8,128)S(1)}, f32[1,256,1536]{2,1,0:T(8,128)}, u32[]{:S(2)}) copy-start(f32[1,256,1536]{2,1,0:T(8,128)} %get-tuple-element.27) | copy-start | bytes 4718596
Sparse Core Ops, SparseCore 0:
  12.0 62.1 all-gather.1
where the time goes:
time: 444 us; the launch traced here: 440 us
  waiting for transfers between devices  240 us (54%)
  other arithmetic  127 us (29%)
  local copies, waits for them, and re-layouts  27 us (6%)
  matrix products  24 us (5%)
  between operations  16.5 us (4%)
  starting transfers between devices  5.3 us (1%)
    ppermute x1, waiting for transfers between devices, swapped(): return lax.ppermute(value, axis, pairs)  177 us
    another operation x15, other arithmetic, body(): factor = jnp.linalg.cholesky(squared)  79.3 us
    all_gather x1, waiting for transfers between devices, body(): own_full = lax.all_gather(mine, 'row', axis=0, tiled=True)  62.4 us
    another operation x3, other arithmetic, body(): solved = jax.scipy.linalg.cho_solve((factor, True), turned).T  41.4 us
    another operation x12, local copies, waits for them, and re-layouts  14 us
  transfers between devices with their start and end apart: 2, of which 2 were waited for; matrix products, arithmetic and copies ran while one was open for 1% of the time, Pallas kernels for 0%

commit v1 on v0

--- a/solution.py
+++ b/solution.py
@@ -22,7 +22,9 @@
     own_index = lax.dynamic_index_in_dim(iface_index, box_id, 0, keepdims=False)
     partner_index = lax.dynamic_index_in_dim(iface_index, partner_id, 0, keepdims=False)
     mine = jnp.take(local[:, outer:], own_index, axis=1)
-    own_full = lax.all_gather(mine, "row", axis=0, tiled=True)
+    own_full = jnp.concatenate(
+        lax.all_to_all(jnp.stack([mine] * lax.axis_size("row")), "row", 0, 0), axis=0
+    )
     other_full = swapped(own_full, "box", 0)
     schur = jnp.take(own_full[outer:], own_index, axis=0) + jnp.take(
         other_full[outer:], partner_index, axis=0

time: 444 us -> 474 us (1.068)
  the two profiles are of different devices: /device:TPU:4 before, /device:TPU:1 now
where the time goes in v1:
time: 474 us; the launch traced here: 470 us
  waiting for transfers between devices  171 us (36%)
  other arithmetic  129 us (27%)
  blocking collectives  103 us (22%)
  local copies, waits for them, and re-layouts  31.4 us (7%)
  matrix products  25.3 us (5%)
  starting transfers between devices  6.5 us (1%)
    ppermute x1, waiting for transfers between devices, swapped(): return lax.ppermute(value, axis, pairs)  171 us
    all_to_all x1, blocking collectives, body(): lax.all_to_all(jnp.stack([mine] * lax.axis_size('row')), 'row', 0, 0)  103 us
    another operation x14, other arithmetic, body(): factor = jnp.linalg.cholesky(squared)  78.8 us
    another operation x3, other arithmetic, body(): solved = jax.scipy.linalg.cho_solve((factor, True), turned).T  41.3 us
    another operation x12, local copies, waits for them, and re-layouts  14.1 us
  transfers between devices with their start and end apart: 1, of which 1 were waited for; matrix products, arithmetic and copies ran while one was open for 2% of the time, Pallas kernels for 0%

profile of v1, /device:TPU:1, one launch (start us, length us, event | category | flops | bytes accessed | tf_op | source)
XLA Modules:
  0.0 470.0 jit_solution(14552358674076919377)
XLA Ops:
  2.0 1.6 gather_fusion
  4.5 103.2 %all_to_all.5 = f32[8,256,512]{2,1,0:T(8,128)} all-to-all(f32[8,256,512]{2,1,0:T(8,128)S(1)} %stack.2), channel_id=1, replica_groups=mesh['box'=64,'row'=8] {'row'}, dimensions={0} | all-to-all | bytes 8388608 | tf_op jit(solution)/shard_map/all_to_all | solution.py:26
  107.7 6.5 %collective-permute-start = (f32[2048,512]{1,0:T(8,128)}, f32[2048,512]{1,0:T(8,128)}, u32[]{:S(2)}, u32[]{:S(2)}) collective-permute-start(f32[2048,512]{1,0:T(8,128)} %bitcast.9), channel_id=1, source_target_pairs={{0,8},{8,0},{16,24},{24,16},{32,40},{40,32},{48,56},{56,48},{64,72... | collective-permute-start | bytes 12582920 | tf_op jit(solution)/shard_map/ppermute | solution.py:10
  115.1 1.9 select_bitcast_fusion.1
  116.9 1.3 slice.200
  118.2 1.6 gather_fusion.1
  119.9 4.2 slice.202
  124.1 171.4 %collective-permute-done = f32[2048,512]{1,0:T(8,128)} collective-permute-done((f32[2048,512]{1,0:T(8,128)}, f32[2048,512]{1,0:T(8,128)}, u32[]{:S(2)}, u32[]{:S(2)}) %collective-permute-start) | collective-permute-done | bytes 4194336 | tf_op jit(solution)/shard_map/ppermute | solution.py:10
  295.5 1.3 slice.201
  296.8 2.1 gather_fusion.2
  299.0 2.2 fusion.58
  301.2 1.3 copy.8
  302.5 1.4 fusion.1
  304.9 11.7 %cholesky.104 = f32[128,128]{1,0:T(8,128)S(1)} custom-call(f32[128,128]{1,0:T(8,128)S(1)} %cholesky.266), custom_call_target="Cholesky" | custom-call | tf_op jit(solution)/shard_map/jit(cholesky)/cholesky | solution.py:33
  316.8 9.8 %custom-call.34 = f32[1,128,128]{1,2,0:T(8,128)S(1)} custom-call(f32[1,128,128]{2,1,0:T(8,128)S(1)} %get-tuple-element.39), custom_call_target="InvertDiagBlocksLowerTriangular" | custom-call | tf_op jit(solution)/shard_map/jit(cholesky)/cholesky | solution.py:33
  329.1 11.9 %cholesky.217 = f32[128,128]{1,0:T(8,128)S(1)} custom-call(f32[128,128]{1,0:T(8,128)S(1)} %cholesky.270), custom_call_target="Cholesky" | custom-call | tf_op jit(solution)/shard_map/jit(cholesky)/cholesky | solution.py:33
  341.0 9.8 %custom-call.35 = f32[1,128,128]{1,2,0:T(8,128)S(1)} custom-call(f32[1,128,128]{2,1,0:T(8,128)S(1)} %get-tuple-element.36), custom_call_target="InvertDiagBlocksLowerTriangular" | custom-call | tf_op jit(solution)/shard_map/jit(cholesky)/cholesky | solution.py:33
  351.1 1.3 convolution_subtract_fusion.5
  352.4 11.7 %cholesky.238 = f32[128,128]{1,0:T(8,128)S(1)} custom-call(f32[128,128]{1,0:T(8,128)S(1)} %cholesky.275), custom_call_target="Cholesky" | custom-call | tf_op jit(solution)/shard_map/jit(cholesky)/cholesky | solution.py:33
  364.8 9.8 %custom-call.36 = f32[1,128,128]{1,2,0:T(8,128)S(1)} custom-call(f32[1,128,128]{2,1,0:T(8,128)S(1)} %get-tuple-element.33), custom_call_target="InvertDiagBlocksLowerTriangular" | custom-call | tf_op jit(solution)/shard_map/jit(cholesky)/cholesky | solution.py:33
  376.1 11.9 %cholesky.255 = f32[128,128]{1,0:T(8,128)S(1)} custom-call(f32[128,128]{1,0:T(8,128)S(1)} %convolution_subtract_fusion.8), custom_call_target="Cholesky" | custom-call | tf_op jit(solution)/shard_map/jit(cholesky)/cholesky | solution.py:33
  393.1 14.1 %while.1 = (s32[]{:T(128)}, f32[512,512]{1,0:T(8,128)}, s32[4,2]{0,1:T(2,128)S(1)}, f32[4,128,128]{2,1,0:T(8,128)}, s32[]{:T(128)}) while((s32[]{:T(128)}, f32[512,512]{1,0:T(8,128)}, s32[4,2]{0,1:T(2,128)S(1)}, f32[4,128,128]{2,1,0:T(8,128)}, s32[]{:T(128)}) %tuple.31), condition=%wide.while_cond, body=%wide.while_body.sunk | while | flops 2 | bytes 132705 | solution.py:46
  393.7 2.9 bitcast_dynamic-update-slice_fusion.2
  397.3 2.9 bitcast_dynamic-update-slice_fusion.2
  400.8 2.9 bitcast_dynamic-update-slice_fusion.2
  404.3 2.8 bitcast_dynamic-update-slice_fusion.2
  407.2 40.2 %custom-call.37 = f32[4,128,128]{1,2,0:T(8,128)S(1)} custom-call(f32[4,128,128]{2,1,0:T(8,128)} %get-tuple-element.13), custom_call_target="InvertDiagBlocksLowerTriangular" | custom-call | tf_op jit(solution)/shard_map/jit(_cho_solve)/triangular_solve | solution.py:46
  447.4 2.3 fusion.2
  454.2 3.0 bitcast_select_fusion.1
  457.3 5.3 %convolution_bitcast_fusion.1 = f32[1,256,1536]{2,1,0:T(8,128)S(1)} fusion(f32[1536,512]{1,0:T(8,128)S(1)} %get-tuple-element.26, f32[128,256]{1,0:T(8,128)S(1)} %fusion.49, f32[128,256]{1,0:T(8,128)S(1)} %fusion.47, f32[128,256]{1,0:T(8,128)S(1)} %fusion.45, f32[128,256]{1,0:T(8,128)S(1)} %fusion.44), kind=kOutput, calls=%fused_computation.10 | convolution fusion | flops 2416312320 | bytes 5242880 | tf_op jit(solution)/shard_map/dot_general | solution.py:48
  462.7 5.6 %convolution_bitcast_fusion = f32[1,256,1536]{2,1,0:T(8,128)S(1)} fusion(f32[1536,512]{1,0:T(8,128)S(1)} %get-tuple-element.27, f32[128,256]{1,0:T(8,128)S(1)} %fusion.49, f32[128,256]{1,0:T(8,128)S(1)} %fusion.47, f32[128,256]{1,0:T(8,128)S(1)} %fusion.45, f32[128,256]{1,0:T(8,128)S(1)} %fusion.44), kind=kOutput, calls=%fused_computation.9 | convolution fusion | flops 2416312320 | bytes 5242880 | tf_op jit(solution)/shard_map/dot_general | solution.py:49
  468.3 1.5 fusion
  (73 shorter events, 19.3 us)
Async XLA Ops:
  3.6 0.9 copy-start.3
  4.5 110.6 %copy-start.6 = (f32[1,256,2048]{2,1,0:T(8,128)S(1)}, f32[1,256,2048]{2,1,0:T(8,128)}, u32[]{:S(2)}) copy-start(f32[1,256,2048]{2,1,0:T(8,128)} %param.4) | copy-start | bytes 6291460
  107.7 187.9 %collective-permute-start = (f32[2048,512]{1,0:T(8,128)}, f32[2048,512]{1,0:T(8,128)}, u32[]{:S(2)}, u32[]{:S(2)}) collective-permute-start(f32[2048,512]{1,0:T(8,128)} %bitcast.9), channel_id=1, source_target_pairs={{0,8},{8,0},{16,24},{24,16},{32,40},{40,32},{48,56},{56,48},{64,72... | collective-permute-start | bytes 12582920 | tf_op jit(solution)/shard_map/ppermute | solution.py:10
  303.9 1.0 copy-start.5
  407.2 42.8 %copy-start.4 = (f32[512,512]{1,0:T(8,128)S(1)}, f32[512,512]{1,0:T(8,128)}, u32[]{:S(2)}) copy-start(f32[512,512]{1,0:T(8,128)} %get-tuple-element.88) | copy-start | bytes 3145732
  450.0 4.2 copy-start
  462.6 5.6 %copy-start.1 = (f32[1,256,1536]{2,1,0:T(8,128)S(1)}, f32[1,256,1536]{2,1,0:T(8,128)}, u32[]{:S(2)}) copy-start(f32[1,256,1536]{2,1,0:T(8,128)} %get-tuple-element.28) | copy-start | bytes 4718596
  462.6 5.6 %copy-start.2 = (f32[1,256,1536]{2,1,0:T(8,128)S(1)}, f32[1,256,1536]{2,1,0:T(8,128)}, u32[]{:S(2)}) copy-start(f32[1,256,1536]{2,1,0:T(8,128)} %get-tuple-element.29) | copy-start | bytes 4718596
